TPU v7x, 128 devices: a whole 4x4x4 slice. The times are simulated.
128 devices in a mesh: row: 8 (over y, core), col: 16 (over z, x).
Axes of the slice: x: 4, y: 4, z: 4, core: 2. Of those that a mesh axis runs over, the one named last changes fastest.
Arguments:
- forward_head: bfloat16 [4, 2048, 1000], P(None, 'col'), may hold values from -6 to 6
- forward_tail: bfloat16 [57344, 1000], P(('col', 'row')), may hold values from -6 to 6
- forward_inverse: bfloat16 [4, 2048, 2048], P(None, 'col', 'row'), may hold values from -1.5 to 1.5, as said below
- forward_coupling: bfloat16 [6, 2048, 2048], P(None, 'row', 'col'), may hold values from -0.078125 to 0.078125
- forward_slab: bfloat16 [4, 2048, 57344], P(None, 'row', 'col'), may hold values from -0.0625 to 0.0625
- backward_head: bfloat16 [4, 2048, 1000], P(None, 'row'), may hold values from -6 to 6
- backward_tail: bfloat16 [57344, 1000], P(('row', 'col')), may hold values from -6 to 6
- backward_inverse: bfloat16 [4, 2048, 2048], P(None, 'col', 'row'), may hold values from -1.5 to 1.5, as said below
- backward_coupling: bfloat16 [6, 2048, 2048], P(None, 'row', 'col'), may hold values from -0.078125 to 0.078125
- backward_slab: bfloat16 [57344, 4, 2048], P('row', None, 'col'), may hold values from -0.0625 to 0.0625
Outputs:
- lower_head: bfloat16 [4, 2048, 1000], P(None, 'row')
- lower_tail: bfloat16 [57344, 1000], P(('col', 'row'))
- upper_head: bfloat16 [4, 2048, 1000], P(None, 'col')
- upper_tail: bfloat16 [57344, 1000], P(('row', 'col'))
Inputs may be any that keep to these rules, and one draw needn't show every extreme that they name: Each block of forward_inverse is upper triangular with diagonal entries of magnitude 0.5 to 1.5. Each block of backward_inverse is upper triangular with diagonal entries of magnitude 0.5 to 1.5.
All inputs are finite; a program needn't handle non-finite values.
Results may differ from a plain program's by a relative error of at most 0.03.
Values may be sent and summed in bfloat16 or wider, within the bound.
No kernel may reach another device: no remote copies, remote signals or barrier semaphores. Data moves between devices by JAX's collectives and lax.ppermute only.
A program may use at most 192 MiB of HBM per device.

v0:
```python
import jax
import jax.numpy as jnp
from jax import lax
from jax.sharding import PartitionSpec as P


def reduce_row(value):
    return lax.psum(value.astype(jnp.bfloat16), "row").astype(jnp.float32)


def reduce_col(value):
    return lax.psum(value.astype(jnp.bfloat16), "col").astype(jnp.float32)


def leading_dot(left, right):
    return lax.dot_general(
        left, right, (((0,), (0,)), ((), ())), preferred_element_type=jnp.float32
    )


def local(
    forward_head,
    forward_tail,
    forward_inverse,
    forward_coupling,
    forward_slab,
    backward_head,
    backward_tail,
    backward_inverse,
    backward_coupling,
    backward_slab,
):
    classes = forward_head.shape[2]
    panels = forward_head.shape[0]
    lower_list = []
    for panel_index in range(panels):
        if panel_index == 0:
            adjusted = forward_head[0]
        else:
            summed = leading_dot(
                forward_coupling[panel_index * (panel_index - 1) // 2], lower_list[0]
            )
            for earlier in range(1, panel_index):
                summed = summed + leading_dot(
                    forward_coupling[panel_index * (panel_index - 1) // 2 + earlier],
                    lower_list[earlier],
                )
            coupling = reduce_row(summed)
            adjusted = (forward_head[panel_index].astype(jnp.float32) - coupling).astype(
                jnp.bfloat16
            )
        lower_list.append(
            reduce_col(leading_dot(forward_inverse[panel_index], adjusted)).astype(jnp.bfloat16)
        )
    lower_head = jnp.stack(lower_list)
    panel_rows = lower_head.shape[1]
    flat_lower = lower_head.reshape(panels * panel_rows, classes)
    flat_slab = forward_slab.reshape(panels * panel_rows, forward_slab.shape[2])
    lower_update = lax.psum_scatter(
        leading_dot(flat_slab, flat_lower).astype(jnp.bfloat16),
        "row",
        scatter_dimension=0,
        tiled=True,
    ).astype(jnp.float32)
    lower_tail = (forward_tail.astype(jnp.float32) - lower_update).astype(jnp.bfloat16)
    upper_list = [None] * panels
    for panel_index in reversed(range(panels)):
        if panel_index == panels - 1:
            shifted = backward_head[panel_index]
        else:
            summed = None
            for later_panel in range(panel_index + 1, panels):
                block = backward_coupling[later_panel * (later_panel - 1) // 2 + panel_index]
                product = jnp.dot(
                    block, upper_list[later_panel], preferred_element_type=jnp.float32
                )
                summed = product if summed is None else summed + product
            pulled = reduce_col(summed)
            shifted = (backward_head[panel_index].astype(jnp.float32) - pulled).astype(jnp.bfloat16)
        upper_list[panel_index] = reduce_row(
            jnp.dot(backward_inverse[panel_index], shifted, preferred_element_type=jnp.float32)
        ).astype(jnp.bfloat16)
    upper_head = jnp.stack(upper_list)
    panel_cols = upper_head.shape[1]
    flat_back = backward_slab.reshape(backward_slab.shape[0], panels * panel_cols)
    flat_upper = upper_head.reshape(panels * panel_cols, classes)
    upper_update = lax.psum_scatter(
        jnp.dot(flat_back, flat_upper, preferred_element_type=jnp.float32).astype(jnp.bfloat16),
        "col",
        scatter_dimension=0,
        tiled=True,
    ).astype(jnp.float32)
    upper_tail = (backward_tail.astype(jnp.float32) - upper_update).astype(jnp.bfloat16)
    return (lower_head, lower_tail, upper_head, upper_tail)


def solution(mesh):
    in_specs = (
        P(None, "col", None),
        P(("col", "row"), None),
        P(None, "col", "row"),
        P(None, "row", "col"),
        P(None, "row", "col"),
        P(None, "row", None),
        P(("row", "col"), None),
        P(None, "col", "row"),
        P(None, "row", "col"),
        P("row", None, "col"),
    )
    out_specs = (
        P(None, "row", None),
        P(("col", "row"), None),
        P(None, "col", None),
        P(("row", "col"), None),
    )
    return jax.shard_map(local, mesh=mesh, in_specs=in_specs, out_specs=out_specs, check_vma=False)
```

profile of v0, /device:TPU:1, one launch (start us, length us, event | category | flops | bytes accessed | tf_op | source)
XLA Modules:
  0.0 793.8 jit_solution(13138176544723374713)
XLA Ops:
  7.2 0.0 all-reduce.15.cloned.1.call-start
  7.2 2.2 convolution_convert_fusion.4
  9.4 0.0 all-reduce.15.cloned.1.call-update
  9.4 0.0 all-reduce.29.cloned.1.call-start
  9.5 2.1 convolution_convert_fusion.8
  11.6 87.5 %all-reduce.15.cloned.1.call-done = bf16[256,1000]{0,1:T(8,128)(2,1)} async-done(((bf16[256,1000]{0,1:T(8,128)(2,1)}), bf16[256,1000]{0,1:T(8,128)(2,1)}) %all-reduce.15.cloned.1.call-update) | async-done | bytes 512016 | tf_op jit(solution)/shard_map/psum | solution.py:12
  99.2 2.1 fusion.13
  101.3 0.0 all-reduce.29.cloned.1.call-update
  101.3 0.0 all-reduce.23.cloned.1.call-start
  101.3 60.2 %all-reduce.29.cloned.1.call-done = (bf16[128,1000]{0,1:T(8,128)(2,1)}, bf16[128,1000]{0,1:T(8,128)(2,1)}) async-done(((bf16[128,1000]{0,1:T(8,128)(2,1)}, bf16[128,1000]{0,1:T(8,128)(2,1)}), (bf16[128,1000]{0,1:T(8,128)(2,1)}, bf16[128,1000]{0,1:T(8,128)(2,1)})) %all-reduce.29.cloned.1.call-update) | async-done | bytes 512016 | tf_op jit(solution)/shard_map/psum | solution.py:8
  161.6 2.0 fusion.7
  163.6 2.1 fusion.10
  165.7 0.0 all-reduce.23.cloned.1.call-update
  165.7 0.0 all-reduce.27.cloned.1.call-start
  165.8 0.3 fusion.66
  166.0 86.8 %all-reduce.23.cloned.1.call-done = (bf16[256,1000]{0,1:T(8,128)(2,1)}, bf16[256,1000]{0,1:T(8,128)(2,1)}) async-done(((bf16[256,1000]{0,1:T(8,128)(2,1)}, bf16[256,1000]{0,1:T(8,128)(2,1)}), (bf16[256,1000]{0,1:T(8,128)(2,1)}, bf16[256,1000]{0,1:T(8,128)(2,1)})) %all-reduce.23.cloned.1.call-update) | async-done | bytes 1024016 | tf_op jit(solution)/shard_map/psum | solution.py:12
  252.8 2.2 fusion.14
  255.1 2.0 fusion.18
  257.1 0.0 all-reduce.27.cloned.1.call-update
  257.1 0.0 all-reduce.21.cloned.1.call-start
  257.2 59.3 %all-reduce.27.cloned.1.call-done = (bf16[128,1000]{0,1:T(8,128)(2,1)}, bf16[128,1000]{0,1:T(8,128)(2,1)}) async-done(((bf16[128,1000]{0,1:T(8,128)(2,1)}, bf16[128,1000]{0,1:T(8,128)(2,1)}), (bf16[128,1000]{0,1:T(8,128)(2,1)}, bf16[128,1000]{0,1:T(8,128)(2,1)})) %all-reduce.27.cloned.1.call-update) | async-done | bytes 512016 | tf_op jit(solution)/shard_map/psum | solution.py:8
  316.5 1.3 fusion.54
  317.8 1.1 fusion.6
  318.9 1.1 fusion.8
  320.0 0.0 all-reduce.21.cloned.1.call-update
  320.0 0.0 all-reduce.25.cloned.1.call-start
  320.1 0.3 fusion.62
  320.4 0.3 convolution_add_fusion.4
  320.7 87.0 %all-reduce.21.cloned.1.call-done = (bf16[256,1000]{0,1:T(8,128)(2,1)}, bf16[256,1000]{0,1:T(8,128)(2,1)}) async-done(((bf16[256,1000]{0,1:T(8,128)(2,1)}, bf16[256,1000]{0,1:T(8,128)(2,1)}), (bf16[256,1000]{0,1:T(8,128)(2,1)}, bf16[256,1000]{0,1:T(8,128)(2,1)})) %all-reduce.21.cloned.1.call-update) | async-done | bytes 1024016 | tf_op jit(solution)/shard_map/psum | solution.py:12
  407.7 2.2 fusion.15
  409.9 2.0 fusion.17
  411.9 0.0 all-reduce.25.cloned.1.call-update
  412.0 0.0 all-reduce.19.cloned.1.call-start
  412.0 59.3 %all-reduce.25.cloned.1.call-done = (bf16[128,1000]{0,1:T(8,128)(2,1)}, bf16[128,1000]{0,1:T(8,128)(2,1)}) async-done(((bf16[128,1000]{0,1:T(8,128)(2,1)}, bf16[128,1000]{0,1:T(8,128)(2,1)}), (bf16[128,1000]{0,1:T(8,128)(2,1)}, bf16[128,1000]{0,1:T(8,128)(2,1)})) %all-reduce.25.cloned.1.call-update) | async-done | bytes 512016 | tf_op jit(solution)/shard_map/psum | solution.py:8
  471.3 1.3 fusion.50
  472.6 1.2 convolution_add_fusion.1
  473.8 2.0 fusion.5
  475.8 2.0 fusion.9
  477.8 0.0 all-reduce.17.cloned.1.call-start
  477.8 87.1 %all-reduce.19.cloned.1.call-done = (bf16[1,256,1000]{1,2,0:T(8,128)(2,1)}, bf16[256,1000]{0,1:T(8,128)(2,1)}) async-done(((bf16[1,256,1000]{1,2,0:T(8,128)(2,1)}, bf16[256,1000]{0,1:T(8,128)(2,1)}), (bf16[1,256,1000]{1,2,0:T(8,128)(2,1)}, bf16[256,1000]{0,1:T(8,128)(2,1)})) %all-reduce.19.cloned.1.call-update) | async-done | bytes 1024016 | tf_op jit(solution)/shard_map/psum | solution.py:12
  565.0 2.2 fusion.16
  567.2 0.0 reduce-scatter.7.cloned.1.call-start
  567.2 1.3 pad_maximum_fusion
  568.6 1.3 copy-done.4
  569.8 12.5 %fusion.2 = bf16[3584,1000]{0,1:T(8,128)(2,1)} fusion(bf16[4,256,1000]{1,2,0:T(8,128)(2,1)S(1)} %pad_maximum_fusion, bf16[4,256,3584]{2,1,0:T(8,128)(2,1)} %param.14), kind=kOutput, calls=%fused_computation.4 | convolution fusion | flops 7343616000 | bytes 16556032 | tf_op jit(solution)/shard_map/dot_general | solution.py:16
  582.4 10.3 %copy.24 = bf16[3584,1000]{1,0:T(8,128)(2,1)} copy(bf16[3584,1000]{0,1:T(8,128)(2,1)} %fusion.2) | data formatting | bytes 14336000
  592.8 0.2 reduce-scatter.9.cloned.1.call-start
  593.0 33.0 %all-reduce.17.cloned.1.call-done = bf16[1,128,1000]{1,2,0:T(8,128)(2,1)} async-done(((bf16[1,128,1000]{1,2,0:T(8,128)(2,1)}), bf16[1,128,1000]{1,2,0:T(8,128)(2,1)}) %all-reduce.17.cloned.1.call-update) | async-done | bytes 256016 | tf_op jit(solution)/shard_map/psum | solution.py:8
  626.0 1.1 pad_maximum_fusion.1
  627.1 0.9 copy-done.6
  628.1 13.4 %fusion = bf16[7168,1000]{0,1:T(8,128)(2,1)} fusion(bf16[4,128,1000]{1,2,0:T(8,128)(2,1)S(1)} %pad_maximum_fusion.1, bf16[7168,4,128]{2,1,0:T(4,128)(2,1)} %param.19), kind=kOutput, calls=%fused_computation.2 | convolution fusion | flops 7347200000 | bytes 22700032 | tf_op jit(solution)/shard_map/dot_general | solution.py:88
  641.5 20.0 %copy.26 = bf16[7168,1000]{1,0:T(8,128)(2,1)} copy(bf16[7168,1000]{0,1:T(8,128)(2,1)} %fusion) | data formatting | bytes 28672000
  661.5 1.2 copy-done.9
  662.7 0.7 copy.20
  663.5 0.5 copy-done.10
  663.9 0.7 copy.19
  664.7 12.0 %reduce-scatter.7.cloned.1.call-done = bf16[448,1000]{1,0:T(8,128)(2,1)} async-done(((bf16[3584,1000]{1,0:T(8,128)(2,1)}), bf16[448,1000]{1,0:T(8,128)(2,1)}) %reduce-scatter.7.cloned.1.call-update) | async-done | bytes 896016
  676.7 2.2 copy.25
  678.9 2.6 subtract_convert_fusion.1
  681.5 2.2 copy.22
  683.7 98.0 %reduce-scatter.9.cloned.1.call-done = bf16[448,1000]{1,0:T(8,128)(2,1)} async-done(((bf16[7168,1000]{1,0:T(8,128)(2,1)}), bf16[448,1000]{1,0:T(8,128)(2,1)}) %reduce-scatter.9.cloned.1.call-update) | async-done | bytes 896016
  781.8 1.7 copy.27
  783.4 1.3 subtract_convert_fusion
  784.8 2.2 copy.23
  (32 shorter events, 0.1 us)
Async XLA Ops:
  7.2 154.4 %copy-start.8 = (bf16[4,128,1000]{1,2,0:T(8,128)(2,1)S(1)}, bf16[4,128,1000]{1,2,0:T(8,128)(2,1)}, u32[]{:S(2)}) copy-start(bf16[4,128,1000]{1,2,0:T(8,128)(2,1)} %param.10) | copy-start | bytes 3072004
  7.2 154.4 %copy-start.13 = (bf16[4,128,256]{2,1,0:T(8,128)(2,1)S(1)}, bf16[4,128,256]{2,1,0:T(8,128)(2,1)}, u32[]{:S(2)}) copy-start(bf16[4,128,256]{2,1,0:T(8,128)(2,1)} %param.12) | copy-start | bytes 786436
  7.2 92.0 %copy-start.11 = (bf16[6,256,128]{2,1,0:T(8,128)(2,1)S(1)}, bf16[6,256,128]{2,1,0:T(8,128)(2,1)}, u32[]{:S(2)}) copy-start(bf16[6,256,128]{2,1,0:T(8,128)(2,1)} %param.13) | copy-start | bytes 1179652
  7.2 92.0 %all-reduce.15.cloned.1.call-start = ((), (), s32[]{:S(2)}) async-start(), calls=%async_computation.2 | async-start | bytes 1024000 | tf_op jit(solution)/shard_map/psum | solution.py:12
  9.4 154.2 %copy-start.12 = (bf16[6,256,128]{2,1,0:T(8,128)(2,1)S(1)}, bf16[6,256,128]{2,1,0:T(8,128)(2,1)}, u32[]{:S(2)}) copy-start(bf16[6,256,128]{2,1,0:T(8,128)(2,1)} %param.18) | copy-start | bytes 1179652
  9.4 152.1 %all-reduce.29.cloned.1.call-start = ((), (), s32[]{:S(2)}) async-start(), calls=%async_computation.11 | async-start | bytes 1024000 | tf_op jit(solution)/shard_map/psum | solution.py:8
  99.2 66.6 %copy-start = (bf16[256,1000]{0,1:T(8,128)(2,1)S(1)}, bf16[256,1000]{0,1:T(8,128)(2,1)}, u32[]{:S(2)}) copy-start(bf16[256,1000]{0,1:T(8,128)(2,1)} %all-reduce.15.cloned.1.call-done) | copy-start | bytes 1536004
  101.3 151.6 %all-reduce.23.cloned.1.call-start = ((), (), s32[]{:S(2)}) async-start(), calls=%async_computation.8 | async-start | bytes 2048000 | tf_op jit(solution)/shard_map/psum | solution.py:12
  165.7 150.8 %all-reduce.27.cloned.1.call-start = ((), (), s32[]{:S(2)}) async-start(), calls=%async_computation.10 | async-start | bytes 1024000 | tf_op jit(solution)/shard_map/psum | solution.py:8
  252.8 65.0 %copy-start.2 = (bf16[128,1000]{0,1:T(8,128)(2,1)S(1)}, bf16[128,1000]{0,1:T(8,128)(2,1)}, u32[]{:S(2)}) copy-start(bf16[128,1000]{0,1:T(8,128)(2,1)} %get-tuple-element.23) | copy-start | bytes 768004
  257.1 150.5 %all-reduce.21.cloned.1.call-start = ((), (), s32[]{:S(2)}) async-start(), calls=%async_computation.7 | async-start | bytes 2048000 | tf_op jit(solution)/shard_map/psum | solution.py:12
  316.5 2.5 copy-start.15
  318.9 1.4 copy-start.1
  320.0 151.3 %all-reduce.25.cloned.1.call-start = ((), (), s32[]{:S(2)}) async-start(), calls=%async_computation.9 | async-start | bytes 1024000 | tf_op jit(solution)/shard_map/psum | solution.py:8
  407.7 64.9 %copy-start.3 = (bf16[128,1000]{0,1:T(8,128)(2,1)S(1)}, bf16[128,1000]{0,1:T(8,128)(2,1)}, u32[]{:S(2)}) copy-start(bf16[128,1000]{0,1:T(8,128)(2,1)} %get-tuple-element.21) | copy-start | bytes 768004
  412.0 153.0 %all-reduce.19.cloned.1.call-start = ((), (), s32[]{:S(2)}) async-start(), calls=%async_computation.6 | async-start | bytes 2048000 | tf_op jit(solution)/shard_map/psum | solution.py:12
  472.6 3.2 copy-start.14
  475.8 91.5 %copy-start.5 = (bf16[256,1000]{0,1:T(8,128)(2,1)S(1)}, bf16[256,1000]{0,1:T(8,128)(2,1)}, u32[]{:S(2)}) copy-start(bf16[256,1000]{0,1:T(8,128)(2,1)} %get-tuple-element.14) | copy-start | bytes 1536004
  477.8 148.2 %all-reduce.17.cloned.1.call-start = ((), (), s32[]{:S(2)}) async-start(), calls=%async_computation.3 | async-start | bytes 512000 | tf_op jit(solution)/shard_map/psum | solution.py:8
  567.2 109.5 %reduce-scatter.7.cloned.1.call-start = ((), (), s32[]{:S(2)}) async-start(), calls=%async_computation.4 | async-start | bytes 8257536
  568.5 1.3 copy-start.4
  592.7 33.3 %copy-start.7 = (bf16[128,1000]{0,1:T(8,128)(2,1)S(1)}, bf16[128,1000]{0,1:T(8,128)(2,1)}, u32[]{:S(2)}) copy-start(bf16[128,1000]{0,1:T(8,128)(2,1)} %get-tuple-element.19) | copy-start | bytes 768004
  592.8 189.0 %reduce-scatter.9.cloned.1.call-start = ((), (), s32[]{:S(2)}) async-start(), calls=%async_computation.5 | async-start | bytes 15597568
  627.1 1.0 copy-start.6
  661.5 1.2 copy-start.9
  662.7 1.2 copy-start.10
Sparse Core Ops, SparseCore 0:
  11.8 87.2 all-reduce.14
  102.4 59.1 all-reduce.28
  165.8 86.9 all-reduce.22
  257.3 59.1 all-reduce.26
  320.6 86.9 all-reduce.20
  412.1 59.1 all-reduce.24
  477.9 86.9 all-reduce.18
  567.9 58.1 all-reduce.16
  628.6 48.0 reduce-scatter.6
  680.3 101.3 reduce-scatter.8
where the time goes:
time: 795 us; the launch traced here: 794 us
  waiting for transfers between devices  670 us (84%)
  matrix products  58 us (7%)
  local copies, waits for them, and re-layouts  44.1 us (6%)
  between operations  14.3 us (2%)
    psum x4, waiting for transfers between devices, reduce_col(): return lax.psum(value.astype(jnp.bfloat16), 'col').astype(jnp.float32)  348 us
    psum x4, waiting for transfers between devices, reduce_row(): return lax.psum(value.astype(jnp.bfloat16), 'row').astype(jnp.float32)  212 us
    unnamed x12, waiting for transfers between devices  110 us
    unnamed x40, local copies, waits for them, and re-layouts  44.1 us
    dot_general x11, matrix products, leading_dot(): lax.dot_general(left, right, (((0,), (0,)), ((), ())), preferred_element_...  26.8 us
  transfers between devices with their start and end apart: 10, of which 10 were waited for; matrix products, arithmetic and copies ran while one was open for 9% of the time, Pallas kernels for 0%

commit v1 on v0

--- a/solution.py
+++ b/solution.py
@@ -9,7 +9,12 @@
 
 
 def reduce_col(value):
-    return lax.psum(value.astype(jnp.bfloat16), "col").astype(jnp.float32)
+
+    def open_the_classes(my_data, chip_axis):
+        odd = lax.all_gather(my_data, chip_axis).sum(axis=0)
+        return odd
+
+    return open_the_classes(value.astype(jnp.bfloat16), "col").astype(jnp.float32)
 
 
 def leading_dot(left, right):

time: 795 us -> 964 us (1.21); the launches traced: 794 us -> 953 us
  waiting for transfers between devices: 670 us -> 747 us
  local copies, waits for them, and re-layouts: 44.1 us -> 87.7 us
  other arithmetic: 6.27 us -> 37.6 us
    all_gather x0 -> x7, waiting for transfers between devices: none -> 398 us  [open_the_classes(): odd = lax.all_gather(my_data, chip_axis).sum(axis=0)]
    psum x4 -> x0, waiting for transfers between devices: 348 us -> none  [reduce_col(): return lax.psum(value.astype(jnp.bfloat16), 'col').astype(jnp.float32)]
    unnamed x40 -> x45, local copies, waits for them, and re-layouts: 44.1 us -> 87.7 us
    reduce_sum x0 -> x7, other arithmetic: none -> 34.4 us  [open_the_classes(): odd = lax.all_gather(my_data, chip_axis).sum(axis=0)]
    psum x4, waiting for transfers between devices: 212 us -> 238 us  [reduce_row(): return lax.psum(value.astype(jnp.bfloat16), 'row').astype(jnp.float32)]
    unnamed x12 -> x15, waiting for transfers between devices: 110 us -> 110 us
  transfers between devices with their start and end apart: 10 -> 13, of which waited for: 10 -> 13; matrix products, arithmetic and copies ran while one was open for 9% -> 14% of each run, Pallas kernels for 0% -> 0%
where the time goes in v1:
time: 964 us; the launch traced here: 953 us
  waiting for transfers between devices  747 us (77%)
  local copies, waits for them, and re-layouts  87.7 us (9%)
  matrix products  64 us (7%)
  other arithmetic  37.6 us (4%)
  between operations  16 us (2%)
    all_gather x7, waiting for transfers between devices, open_the_classes(): odd = lax.all_gather(my_data, chip_axis).sum(axis=0)  398 us
    psum x4, waiting for transfers between devices, reduce_row(): return lax.psum(value.astype(jnp.bfloat16), 'row').astype(jnp.float32)  238 us
    unnamed x15, waiting for transfers between devices  110 us
    unnamed x45, local copies, waits for them, and re-layouts  87.7 us
    reduce_sum x7, other arithmetic, open_the_classes(): odd = lax.all_gather(my_data, chip_axis).sum(axis=0)  34.4 us
    dot_general x11, matrix products, leading_dot(): lax.dot_general(left, right, (((0,), (0,)), ((), ())), preferred_element_...  32 us
  transfers between devices with their start and end apart: 13, of which 13 were waited for; matrix products, arithmetic and copies ran while one was open for 14% of the time, Pallas kernels for 0%

profile of v1, /device:TPU:1, one launch (start us, length us, event | category | flops | bytes accessed | tf_op | source)
XLA Modules:
  0.0 952.9 jit_solution(1053346349753376828)
XLA Ops:
  8.0 2.1 convolution_convert_fusion.8
  10.2 2.1 convolution_convert_fusion.4
  12.3 61.1 %all-reduce.8.cloned.1.call-done = bf16[128,1000]{0,1:T(8,128)(2,1)} async-done(((bf16[128,1000]{0,1:T(8,128)(2,1)}), bf16[128,1000]{0,1:T(8,128)(2,1)}) %all-reduce.8.cloned.1.call-update) | async-done | bytes 256016 | tf_op jit(solution)/shard_map/psum | solution.py:8
  73.4 2.1 fusion.10
  75.6 16.5 %all-gather.15.cloned.1.call-done = bf16[4096,1000]{0,1:T(8,128)(2,1)} async-done(((bf16[256,1000]{0,1:T(8,128)(2,1)}), bf16[4096,1000]{0,1:T(8,128)(2,1)}) %all-gather.15.cloned.1.call-update) | async-done | bytes 8192016 | tf_op jit(solution)/shard_map/all_gather | solution.py:14
  92.1 6.4 copy.28
  98.5 4.7 bitcast_reduce_fusion.6
  103.2 0.8 copy-done
  104.0 1.8 fusion.13
  105.8 65.1 %all-gather.23.cloned.1.call-done = bf16[4096,1000]{0,1:T(8,128)(2,1)} async-done(((bf16[256,1000]{0,1:T(8,128)(2,1)}), bf16[4096,1000]{0,1:T(8,128)(2,1)}) %all-gather.23.cloned.1.call-update) | async-done | bytes 8192016 | tf_op jit(solution)/shard_map/all_gather | solution.py:14
  170.9 6.4 copy.32
  177.3 5.1 bitcast_reduce_fusion.2
  182.4 2.1 fusion.14
  184.6 59.1 %all-reduce.14.cloned.1.call-done = (bf16[128,1000]{0,1:T(8,128)(2,1)}, bf16[128,1000]{0,1:T(8,128)(2,1)}) async-done(((bf16[128,1000]{0,1:T(8,128)(2,1)}, bf16[128,1000]{0,1:T(8,128)(2,1)}), (bf16[128,1000]{0,1:T(8,128)(2,1)}, bf16[128,1000]{0,1:T(8,128)(2,1)})) %all-reduce.14.cloned.1.call-update) | async-done | bytes 512016 | tf_op jit(solution)/shard_map/psum | solution.py:8
  243.7 2.2 fusion.7
  245.9 1.3 fusion.57
  247.2 2.1 fusion.6
  249.4 1.9 fusion.69
  251.3 71.4 %all-gather.17.cloned.1.call-done = bf16[4096,1000]{0,1:T(8,128)(2,1)} async-done(((bf16[256,1000]{0,1:T(8,128)(2,1)}), bf16[4096,1000]{0,1:T(8,128)(2,1)}) %all-gather.17.cloned.1.call-update) | async-done | bytes 8192016 | tf_op jit(solution)/shard_map/all_gather | solution.py:14
  322.8 6.4 copy.29
  329.1 5.5 bitcast_reduce_fusion.5
  334.6 66.9 %all-gather.25.cloned.1.call-done = bf16[4096,1000]{0,1:T(8,128)(2,1)} async-done(((bf16[256,1000]{0,1:T(8,128)(2,1)}), bf16[4096,1000]{0,1:T(8,128)(2,1)}) %all-gather.25.cloned.1.call-update) | async-done | bytes 8192016 | tf_op jit(solution)/shard_map/all_gather | solution.py:14
  401.5 6.4 copy.33
  407.8 4.9 bitcast_reduce_fusion.1
  412.7 2.1 fusion.15
  414.9 1.8 fusion.18
  416.8 59.1 %all-reduce.12.cloned.1.call-done = (bf16[128,1000]{0,1:T(8,128)(2,1)}, bf16[128,1000]{0,1:T(8,128)(2,1)}) async-done(((bf16[128,1000]{0,1:T(8,128)(2,1)}, bf16[128,1000]{0,1:T(8,128)(2,1)}), (bf16[128,1000]{0,1:T(8,128)(2,1)}, bf16[128,1000]{0,1:T(8,128)(2,1)})) %all-reduce.12.cloned.1.call-update) | async-done | bytes 512016 | tf_op jit(solution)/shard_map/psum | solution.py:8
  475.9 1.3 fusion.53
  477.2 1.3 convolution_add_fusion.1
  478.5 2.1 fusion.5
  480.7 2.2 fusion.8
  482.9 1.1 fusion.65
  484.1 1.9 convolution_add_fusion.4
  486.0 71.5 %all-gather.27.cloned.1.call-done = bf16[4096,1000]{0,1:T(8,128)(2,1)} async-done(((bf16[256,1000]{0,1:T(8,128)(2,1)}), bf16[4096,1000]{0,1:T(8,128)(2,1)}) %all-gather.27.cloned.1.call-update) | async-done | bytes 8192016 | tf_op jit(solution)/shard_map/all_gather | solution.py:14
  557.5 6.4 copy.34
  563.9 4.7 bitcast_reduce_fusion
  568.5 2.0 fusion.16
  570.6 65.8 %all-gather.19.cloned.1.call-done = bf16[4096,1000]{0,1:T(8,128)(2,1)} async-done(((bf16[256,1000]{0,1:T(8,128)(2,1)}), bf16[4096,1000]{0,1:T(8,128)(2,1)}) %all-gather.19.cloned.1.call-update) | async-done | bytes 8192016 | tf_op jit(solution)/shard_map/all_gather | solution.py:14
  636.4 6.4 copy.30
  642.8 4.9 bitcast_reduce_fusion.4
  647.7 0.8 copy-done.7
  648.5 1.8 fusion.17
  650.4 59.1 %all-reduce.10.cloned.1.call-done = (bf16[128,1000]{0,1:T(8,128)(2,1)}, bf16[1,128,1000]{1,2,0:T(8,128)(2,1)}) async-done(((bf16[128,1000]{0,1:T(8,128)(2,1)}, bf16[1,128,1000]{1,2,0:T(8,128)(2,1)}), (bf16[128,1000]{0,1:T(8,128)(2,1)}, bf16[1,128,1000]{1,2,0:T(8,128)(2,1)})) %all-reduce.10.cloned.1.call-update) | async-done | bytes 512016 | tf_op jit(solution)/shard_map/psum | solution.py:8
  709.5 2.2 fusion.9
  711.7 1.5 pad_maximum_fusion.1
  713.2 0.9 copy-done.12
  714.1 13.5 %fusion = bf16[7168,1000]{0,1:T(8,128)(2,1)} fusion(bf16[4,128,1000]{1,2,0:T(8,128)(2,1)S(1)} %pad_maximum_fusion.1, bf16[7168,4,128]{2,1,0:T(4,128)(2,1)} %param.19), kind=kOutput, calls=%fused_computation.2 | convolution fusion | flops 7347200000 | bytes 22700032 | tf_op jit(solution)/shard_map/dot_general | solution.py:93
  727.7 19.8 %copy.26 = bf16[7168,1000]{1,0:T(8,128)(2,1)} copy(bf16[7168,1000]{0,1:T(8,128)(2,1)} %fusion) | data formatting | bytes 28672000
  747.5 0.4 reduce-scatter.7.cloned.1.call-start
  748.0 40.5 %all-gather.21.cloned.1.call-done = bf16[4096,1000]{0,1:T(8,128)(2,1)} async-done(((bf16[256,1000]{0,1:T(8,128)(2,1)}), bf16[4096,1000]{0,1:T(8,128)(2,1)}) %all-gather.21.cloned.1.call-update) | async-done | bytes 8192016 | tf_op jit(solution)/shard_map/all_gather | solution.py:14
  788.5 6.4 copy.31
  794.9 4.7 bitcast_reduce_fusion.3
  799.9 1.3 copy-done.9
  801.2 12.9 %fusion.2 = bf16[3584,1000]{0,1:T(8,128)(2,1)} fusion(bf16[4,256,1000]{1,2,0:T(8,128)(2,1)S(1)} %pad_maximum_fusion, bf16[4,256,3584]{2,1,0:T(8,128)(2,1)} %param.14), kind=kOutput, calls=%fused_computation.11 | convolution fusion | flops 7343616000 | bytes 16556032 | tf_op jit(solution)/shard_map/dot_general | solution.py:21
  814.2 10.6 %copy.24 = bf16[3584,1000]{1,0:T(8,128)(2,1)} copy(bf16[3584,1000]{0,1:T(8,128)(2,1)} %fusion.2) | data formatting | bytes 14336000
  824.8 0.7 copy.20
  826.0 0.7 copy.19
  826.7 66.9 %reduce-scatter.9.cloned.1.call-done = bf16[448,1000]{1,0:T(8,128)(2,1)} async-done(((bf16[7168,1000]{1,0:T(8,128)(2,1)}), bf16[448,1000]{1,0:T(8,128)(2,1)}) %reduce-scatter.9.cloned.1.call-update) | async-done | bytes 896016
  893.7 1.7 copy.27
  895.3 1.3 subtract_convert_fusion
  896.6 2.2 copy.23
  898.8 43.1 %reduce-scatter.7.cloned.1.call-done = bf16[448,1000]{1,0:T(8,128)(2,1)} async-done(((bf16[3584,1000]{1,0:T(8,128)(2,1)}), bf16[448,1000]{1,0:T(8,128)(2,1)}) %reduce-scatter.7.cloned.1.call-update) | async-done | bytes 896016
  942.0 1.7 copy.25
  943.9 1.4 copy.22
  (53 shorter events, 1.8 us)
Async XLA Ops:
  8.0 65.5 %all-reduce.8.cloned.1.call-start = ((), (), s32[]{:S(2)}) async-start(), calls=%async_computation.2 | async-start | bytes 512000 | tf_op jit(solution)/shard_map/psum | solution.py:8
  10.1 82.0 %all-gather.15.cloned.1.call-start = ((), (), s32[]{:S(2)}) async-start(), calls=%async_computation.3 | async-start | bytes 8704000 | tf_op jit(solution)/shard_map/all_gather | solution.py:14
  12.3 158.6 %all-gather.23.cloned.1.call-start = ((), (), s32[]{:S(2)}) async-start(), calls=%async_computation.7 | async-start | bytes 8704000 | tf_op jit(solution)/shard_map/all_gather | solution.py:14
  75.6 168.1 %all-reduce.14.cloned.1.call-start = ((), (), s32[]{:S(2)}) async-start(), calls=%async_computation.14 | async-start | bytes 1024000 | tf_op jit(solution)/shard_map/psum | solution.py:8
  103.2 0.8 copy-start
  182.4 67.0 %copy-start.1 = (bf16[256,1000]{0,1:T(8,128)(2,1)S(1)}, bf16[256,1000]{0,1:T(8,128)(2,1)}, u32[]{:S(2)}) copy-start(bf16[256,1000]{0,1:T(8,128)(2,1)} %copy-done) | copy-start | bytes 1536004
  184.5 138.2 %all-gather.17.cloned.1.call-start = ((), (), s32[]{:S(2)}) async-start(), calls=%async_computation.4 | async-start | bytes 8704000 | tf_op jit(solution)/shard_map/all_gather | solution.py:14
  245.9 155.6 %all-gather.25.cloned.1.call-start = ((), (), s32[]{:S(2)}) async-start(), calls=%async_computation.8 | async-start | bytes 8704000 | tf_op jit(solution)/shard_map/all_gather | solution.py:14
  249.3 226.6 %all-reduce.12.cloned.1.call-start = ((), (), s32[]{:S(2)}) async-start(), calls=%async_computation.13 | async-start | bytes 1024000 | tf_op jit(solution)/shard_map/psum | solution.py:8
  407.8 7.0 copy-start.4
  407.8 7.0 copy-start.11
  412.7 70.2 %copy-start.2 = (bf16[256,1000]{0,1:T(8,128)(2,1)S(1)}, bf16[256,1000]{0,1:T(8,128)(2,1)}, u32[]{:S(2)}) copy-start(bf16[256,1000]{0,1:T(8,128)(2,1)} %copy-done) | copy-start | bytes 1536004
  412.7 71.3 %copy-start.5 = (bf16[256,1000]{0,1:T(8,128)(2,1)S(1)}, bf16[256,1000]{0,1:T(8,128)(2,1)}, u32[]{:S(2)}) copy-start(bf16[256,1000]{0,1:T(8,128)(2,1)} %bitcast_reduce_fusion.5) | copy-start | bytes 1536004
  416.7 140.8 %all-gather.27.cloned.1.call-start = ((), (), s32[]{:S(2)}) async-start(), calls=%async_computation.9 | async-start | bytes 8704000 | tf_op jit(solution)/shard_map/all_gather | solution.py:14
  480.6 155.8 %all-gather.19.cloned.1.call-start = ((), (), s32[]{:S(2)}) async-start(), calls=%async_computation.5 | async-start | bytes 8704000 | tf_op jit(solution)/shard_map/all_gather | solution.py:14
  482.9 226.6 %all-reduce.10.cloned.1.call-start = ((), (), s32[]{:S(2)}) async-start(), calls=%async_computation.12 | async-start | bytes 1024000 | tf_op jit(solution)/shard_map/psum | solution.py:8
  642.8 5.7 copy-start.10
  647.7 0.8 copy-start.7
  650.3 138.2 %all-gather.21.cloned.1.call-start = ((), (), s32[]{:S(2)}) async-start(), calls=%async_computation.6 | async-start | bytes 8704000 | tf_op jit(solution)/shard_map/all_gather | solution.py:14
  711.7 182.0 %reduce-scatter.9.cloned.1.call-start = ((), (), s32[]{:S(2)}) async-start(), calls=%async_computation.11 | async-start | bytes 15597568
  713.2 1.0 copy-start.12
  747.5 194.4 %reduce-scatter.7.cloned.1.call-start = ((), (), s32[]{:S(2)}) async-start(), calls=%async_computation.10 | async-start | bytes 8257536
  794.9 4.7 copy-start.3
  794.9 4.7 copy-start.6
  794.9 4.7 copy-start.8
  799.9 1.3 copy-start.9
  814.2 10.6 %copy-start.13 = (bf16[448,1000]{1,0:T(8,128)(2,1)S(1)}, bf16[448,1000]{1,0:T(8,128)(2,1)}, u32[]{:S(2)}) copy-start(bf16[448,1000]{1,0:T(8,128)(2,1)} %param.16) | copy-start | bytes 2688004
  824.8 1.2 copy-start.14
Sparse Core Ops, SparseCore 0:
  11.7 61.6 all-reduce.7
  184.7 58.9 all-reduce.13
  416.9 59.0 all-reduce.11
  650.4 58.9 all-reduce.9
Sparse Core Ops, SparseCore 1:
  13.3 78.8 all-gather.14
  94.9 75.9 all-gather.22
  246.0 76.7 all-gather.16
  325.5 75.9 all-gather.24
  480.7 76.7 all-gather.26
  560.4 75.9 all-gather.18
  711.7 76.7 all-gather.20
  791.8 101.8 reduce-scatter.8
  895.9 46.0 reduce-scatter.6
